TPU v7x, 32 devices: a whole 2x2x4 slice. The times are simulated.
32 devices in a mesh: dp: 4 (over y, core), mp: 8 (over z, x).
Axes of the slice: x: 2, y: 2, z: 4, core: 2. Of those that a mesh axis runs over, the one named last changes fastest.
Arguments:
- tokens: bfloat16 [512, 6144], P('dp', 'mp'), may hold values from -6 to 6
- norm_gain: bfloat16 [6144], P('mp'), may hold values from 0.5 to 1.5
- qkv_weight: bfloat16 [3, 128, 24, 6144], P(None, 'mp', None, 'dp'), may hold values from -0.078125 to 0.078125
- head_weight: bfloat16 [128, 24, 6144], P('mp', None, 'dp'), may hold values from -0.109375 to 0.109375
- up_weight: bfloat16 [12288, 6144], P('mp', 'dp'), may hold values from -0.078125 to 0.078125
- down_weight: bfloat16 [12288, 6144], P('mp', 'dp'), may hold values from -0.0546875 to 0.0546875
- cotangent: bfloat16 [512, 6144], P('dp', 'mp'), may hold values from -6 to 6
Outputs:
- mixed: bfloat16 [512, 6144], P('dp', 'mp')
- tokens_grad: float32 [512, 6144], P('dp', 'mp')
- qkv_grad: bfloat16 [3, 128, 24, 6144], P(None, 'mp', None, 'dp')
- head_grad: bfloat16 [128, 24, 6144], P('mp', None, 'dp')
- up_grad: bfloat16 [12288, 6144], P('mp', 'dp')
- down_grad: bfloat16 [12288, 6144], P('mp', 'dp')
- gain_grad: float32 [6144], P('mp')
All inputs are finite; a program needn't handle non-finite values.
Results may differ from a plain program's by a relative error of at most 0.013.
Values may be sent and summed in bfloat16 or wider, within the bound.
No kernel may reach another device: no remote copies, remote signals or barrier semaphores. Data moves between devices by JAX's collectives and lax.ppermute only.
A program may use at most 256 MiB of HBM per device.

v0:
```python
import math
import jax
import jax.numpy as jnp
from jax import lax
from jax.sharding import PartitionSpec as P

D = 6144
HEADS = 24
HS = 128
PATCHES = 128
QB = 8
IMG_DP = 1
ROWS = 128
TQ = 16
ITEMS = 192
epsilon = 1e-06
contract_rows = (((0,), (0,)), ((), ()))
contract_cols = (((1,), (1,)), ((), ()))


def gelu_pair(inputs):
    normal_cdf = 0.5 * (1.0 + jax.scipy.special.erf(inputs * 0.7071067811865476))
    density = jnp.exp(-0.5 * inputs * inputs) * 0.3989422804014327
    return (inputs * normal_cdf, normal_cdf + inputs * density)


def head_norm(values):
    center = values - jnp.mean(values, axis=0, keepdims=True)
    inverse = lax.rsqrt(jnp.mean(center * center, axis=0, keepdims=True) + epsilon)
    return (center * inverse, inverse)


def norm_back(upstream, normed, inverse):
    return inverse * (
        upstream
        - jnp.mean(upstream, axis=0, keepdims=True)
        - normed * jnp.mean(upstream * normed, axis=0, keepdims=True)
    )


def to_items(pair_rows):
    depth = pair_rows.shape[1]
    shaped = pair_rows.reshape(2, depth, HEADS, IMG_DP, 1, PATCHES)
    spread = jnp.broadcast_to(shaped, (2, depth, HEADS, IMG_DP, QB, PATCHES))
    return jnp.transpose(spread, (1, 2, 3, 4, 0, 5)).reshape(depth, HEADS * IMG_DP * QB, 2, PATCHES)


def from_items(pair_items):
    depth = pair_items.shape[0]
    shaped = pair_items.reshape(depth, HEADS, IMG_DP, QB, 2, PATCHES)
    summed = jnp.sum(shaped.astype(jnp.float32), axis=3).astype(jnp.bfloat16)
    return jnp.transpose(summed, (3, 0, 1, 2, 4)).reshape(2, depth, HEADS, IMG_DP * PATCHES)


def attend(queries, keyvals):
    query_hat, query_scale = head_norm(queries.astype(jnp.float32))
    key_hat, key_scale = head_norm(keyvals[:, :, 0].astype(jnp.float32))
    query_norm = query_hat.astype(jnp.bfloat16)
    key_norm = key_hat.astype(jnp.bfloat16)
    factor = 1.0 / math.sqrt(queries.shape[0])
    scores = (
        jnp.einsum("cia,cib->iab", query_norm, key_norm, preferred_element_type=jnp.float32)
        * factor
    )
    raised = jnp.exp(scores)
    shares = raised / jnp.sum(raised, axis=2, keepdims=True)
    rounded = shares.astype(jnp.bfloat16)
    values = keyvals[:, :, 1]
    attended = jnp.einsum(
        "iab,cib->cia", rounded, values, preferred_element_type=jnp.float32
    ).astype(jnp.bfloat16)
    stored = (
        query_hat,
        query_scale,
        key_hat,
        key_scale,
        query_norm,
        key_norm,
        shares,
        rounded,
        values,
    )
    return (attended, stored)


def attend_back(upstream, stored):
    query_hat, query_scale, key_hat, key_scale, query_norm, key_norm, shares, rounded, values = (
        stored
    )
    factor = 1.0 / math.sqrt(upstream.shape[0])
    share_grad = jnp.einsum("cia,cib->iab", upstream, values, preferred_element_type=jnp.float32)
    value_grad = jnp.einsum("iab,cia->cib", rounded, upstream, preferred_element_type=jnp.float32)
    score_grad = (
        shares * (share_grad - jnp.sum(shares * share_grad, axis=2, keepdims=True)) * factor
    ).astype(jnp.bfloat16)
    query_back = jnp.einsum(
        "iab,cib->cia", score_grad, key_norm, preferred_element_type=jnp.float32
    )
    key_back = jnp.einsum(
        "iab,cia->cib", score_grad, query_norm, preferred_element_type=jnp.float32
    )
    query_grad = norm_back(query_back, query_hat, query_scale).astype(jnp.bfloat16)
    key_grad = norm_back(key_back, key_hat, key_scale).astype(jnp.bfloat16)
    pair_grad = jnp.stack([key_grad, value_grad.astype(jnp.bfloat16)], axis=2)
    return (query_grad, pair_grad)


def swap_pairs(n_dp, n_mp):
    ratio = n_mp // n_dp
    pairs = []
    for row in range(n_dp):
        for col in range(n_mp):
            owner, part = divmod(col, ratio)
            pairs.append((row * n_mp + col, owner * n_mp + row * ratio + part))
    return pairs


def swap(block):
    n_dp, n_mp = (lax.axis_size("dp"), lax.axis_size("mp"))
    return lax.ppermute(block, ("dp", "mp"), swap_pairs(n_dp, n_mp))


def spread_quarter(block):
    n_dp, n_mp = (lax.axis_size("dp"), lax.axis_size("mp"))
    ratio = n_mp // n_dp
    rows, width = block.shape
    pieces = lax.all_gather(swap(block), "mp", axis=0, tiled=False)
    pieces = pieces.reshape(n_dp, ratio, rows, width)
    return jnp.transpose(pieces, (0, 2, 1, 3)).reshape(n_dp * rows, ratio * width)


def gather_quarter(partial, rows):
    n_dp, n_mp = (lax.axis_size("dp"), lax.axis_size("mp"))
    ratio = n_mp // n_dp
    width = partial.shape[1] // ratio
    pieces = partial.reshape(n_dp, rows, ratio, width)
    pieces = jnp.transpose(pieces, (0, 2, 1, 3)).reshape(n_mp, rows, width)
    summed = lax.psum_scatter(pieces, "mp", scatter_dimension=0, tiled=True)
    return swap(summed.reshape(rows, width))


def blockwise_grad(left, right, n_blocks):
    rows = left.shape[1] // n_blocks
    total = None
    for block in range(n_blocks):
        piece = (
            jnp.dot(
                left[:, block * rows : (block + 1) * rows],
                right[block * rows : (block + 1) * rows],
                preferred_element_type=jnp.float32,
            )
            .astype(jnp.bfloat16)
            .astype(jnp.float32)
        )
        total = piece if total is None else total + piece
    return total.astype(jnp.bfloat16)


def shards(tokens, norm_gain, qkv_weight, head_weight, up_weight, down_weight, cotangent):
    n_dp, n_mp = (lax.axis_size("dp"), lax.axis_size("mp"))
    head_slice = HS // n_mp
    quarter = qkv_weight.shape[-1]
    rows, width = tokens.shape
    qkv_flat = qkv_weight.reshape(-1, quarter)
    head_flat = head_weight.reshape(-1, quarter)
    widened = tokens.astype(jnp.float32)
    block_mean = jnp.mean(widened, axis=1)
    block_center = widened - block_mean[:, None]
    block_m2 = jnp.sum(block_center * block_center, axis=1)
    stats = lax.all_gather(jnp.stack([block_mean, block_m2]), "mp", axis=0, tiled=False)
    row_mean = jnp.mean(stats[:, 0], axis=0)
    spread = stats[:, 0] - row_mean[None, :]
    row_m2 = jnp.sum(stats[:, 1], axis=0) + width * jnp.sum(spread * spread, axis=0)
    row_scale = lax.rsqrt(row_m2 / D + epsilon)[:, None]
    normed = (widened - row_mean[:, None]) * row_scale
    gain_wide = norm_gain.astype(jnp.float32)
    hidden_local = (normed * gain_wide).astype(jnp.bfloat16)
    hidden_all = spread_quarter(hidden_local)
    cot_all = spread_quarter(cotangent)
    projected = lax.dot_general(
        qkv_flat, hidden_all, contract_cols, preferred_element_type=jnp.float32
    )
    projected = lax.psum_scatter(projected, "dp", scatter_dimension=1, tiled=True)
    projected = projected.astype(jnp.bfloat16).reshape(3, head_slice, HEADS, ROWS)
    up_input = lax.dot_general(
        up_weight, hidden_all, contract_cols, preferred_element_type=jnp.float32
    )
    up_input = lax.psum_scatter(up_input, "dp", scatter_dimension=1, tiled=True)
    activated, gelu_slope = gelu_pair(up_input)
    up_output = activated.astype(jnp.bfloat16)
    queries = projected[0].reshape(head_slice, ITEMS, TQ)
    keyvals = to_items(projected[1:])
    query_heads, pair_heads = (
        lax.all_to_all(queries, "mp", split_axis=1, concat_axis=0, tiled=True),
        lax.all_to_all(keyvals, "mp", split_axis=1, concat_axis=0, tiled=True),
    )
    attended, stored = attend(query_heads, pair_heads)
    head_rows = lax.all_to_all(attended, "mp", split_axis=0, concat_axis=1, tiled=True).reshape(
        head_slice * HEADS, ROWS
    )
    head_rows_all = lax.all_gather(head_rows, "dp", axis=1, tiled=True)
    up_output_all = lax.all_gather(up_output, "dp", axis=1, tiled=True)
    branch = lax.dot_general(
        head_rows_all, head_flat, contract_rows, preferred_element_type=jnp.float32
    ) + lax.dot_general(
        up_output_all, down_weight, contract_rows, preferred_element_type=jnp.float32
    )
    branch_local = gather_quarter(branch, rows)
    mixed = (widened + branch_local).astype(jnp.bfloat16)
    down_grad = blockwise_grad(up_output_all, cot_all, n_dp)
    head_grad = blockwise_grad(head_rows_all, cot_all, n_dp)
    up_back = lax.dot_general(
        down_weight, cot_all, contract_cols, preferred_element_type=jnp.float32
    )
    up_back = lax.psum_scatter(up_back, "dp", scatter_dimension=1, tiled=True)
    up_upstream = (up_back * gelu_slope).astype(jnp.bfloat16)
    head_upstream = lax.dot_general(
        head_flat, cot_all, contract_cols, preferred_element_type=jnp.float32
    )
    head_upstream = lax.psum_scatter(head_upstream, "dp", scatter_dimension=1, tiled=True)
    head_upstream = head_upstream.astype(jnp.bfloat16).reshape(head_slice, ITEMS, TQ)
    upstream = lax.all_to_all(head_upstream, "mp", split_axis=1, concat_axis=0, tiled=True)
    query_grad, pair_grad = attend_back(upstream, stored)
    query_local, pair_local = (
        lax.all_to_all(query_grad, "mp", split_axis=0, concat_axis=1, tiled=True),
        lax.all_to_all(pair_grad, "mp", split_axis=0, concat_axis=1, tiled=True),
    )
    proj_grad = jnp.concatenate(
        [query_local.reshape(1, head_slice, HEADS, ROWS), from_items(pair_local)], axis=0
    )
    proj_grad = proj_grad.reshape(3 * head_slice * HEADS, ROWS)
    proj_grad_all = lax.all_gather(proj_grad, "dp", axis=1, tiled=True)
    up_upstream_all = lax.all_gather(up_upstream, "dp", axis=1, tiled=True)
    qkv_grad = blockwise_grad(proj_grad_all, hidden_all, n_dp)
    up_grad = blockwise_grad(up_upstream_all, hidden_all, n_dp)
    input_partial = lax.dot_general(
        proj_grad_all, qkv_flat, contract_rows, preferred_element_type=jnp.float32
    ) + lax.dot_general(
        up_upstream_all, up_weight, contract_rows, preferred_element_type=jnp.float32
    )
    input_local = gather_quarter(input_partial, rows)
    scaled = input_local * gain_wide
    plain_sum, cross_sum = lax.psum(
        (jnp.sum(scaled, axis=1), jnp.sum(scaled * normed, axis=1)), "mp"
    )
    tokens_grad = row_scale * (scaled - plain_sum[:, None] / D - normed * (cross_sum[:, None] / D))
    tokens_grad = tokens_grad + cotangent.astype(jnp.float32)
    gain_piece = jnp.sum(input_local * normed, axis=0)
    gain_grad = lax.psum(gain_piece, "dp")
    return (
        mixed,
        tokens_grad,
        qkv_grad.reshape(qkv_weight.shape),
        head_grad.reshape(head_weight.shape),
        up_grad,
        down_grad,
        gain_grad,
    )


def solution(mesh):
    in_specs = (
        P("dp", "mp"),
        P("mp"),
        P(None, "mp", None, "dp"),
        P("mp", None, "dp"),
        P("mp", "dp"),
        P("mp", "dp"),
        P("dp", "mp"),
    )
    out_specs = (
        P("dp", "mp"),
        P("dp", "mp"),
        P(None, "mp", None, "dp"),
        P("mp", None, "dp"),
        P("mp", "dp"),
        P("mp", "dp"),
        P("mp"),
    )
    return jax.shard_map(shards, mesh=mesh, in_specs=in_specs, out_specs=out_specs, check_vma=False)
```

profile of v0, /device:TPU:0, one launch (start us, length us, event | category | flops | bytes accessed | tf_op | source)
XLA Modules:
  0.0 604.6 jit_solution(15431614046644285964)
XLA Ops:
  13.6 31.0 %all-gather.3 = f32[8,2,128]{2,1,0:T(2,128)S(1)} all-gather(f32[1,2,128]{2,1,0:T(2,128)S(1)} %maximum_bitcast_fusion), channel_id=2, replica_groups=mesh['dp'=4,'mp'=8] {'mp'}, dimensions={0}, use_global_device_ids=true | all-gather | bytes 9216 | tf_op jit(solution)/shard_map/all_gather | solution.py:170
  47.1 21.2 %all-gather.18.cloned.1.call-done = bf16[1024,768]{1,0:T(8,128)(2,1)} async-done(((bf16[128,768]{1,0:T(8,128)(2,1)}), bf16[1024,768]{1,0:T(8,128)(2,1)}) %all-gather.18.cloned.1.call-update) | async-done | bytes 1572880 | tf_op jit(solution)/shard_map/all_gather | solution.py:127
  74.6 40.2 %all-gather.16.cloned.1.call-done = bf16[1024,768]{1,0:T(8,128)(2,1)} async-done(((bf16[128,768]{1,0:T(8,128)(2,1)}), bf16[1024,768]{1,0:T(8,128)(2,1)}) %all-gather.16.cloned.1.call-update) | async-done | bytes 1572880 | tf_op jit(solution)/shard_map/all_gather | solution.py:127
  123.0 7.3 %fusion.110 = f32[1536,512]{0,1:T(8,128)} fusion(bf16[1536,1536]{1,0:T(8,128)(2,1)} %param.12, bf16[512,1536]{1,0:T(8,128)(2,1)} %bitcast.239), kind=kOutput, calls=%fused_computation.162 | convolution fusion | flops 2415919104 | bytes 9437184 | tf_op jit(solution)/shard_map/dot_general | solution.py:212
  130.3 9.7 %reduce-scatter.13.cloned.1.call-done = f32[384,128]{1,0:T(8,128)} async-done(((f32[384,512]{1,0:T(8,128)}), f32[384,128]{1,0:T(8,128)}) %reduce-scatter.13.cloned.1.call-update) | async-done | bytes 196624 | tf_op jit(solution)/shard_map/reduce_scatter | solution.py:220
  149.0 5.5 all-to-all-start.3
  154.5 21.7 %reduce-scatter.7.cloned.1.call-done = f32[1152,128]{0,1:T(8,128)} async-done(((f32[1152,512]{0,1:T(8,128)}), f32[1152,128]{0,1:T(8,128)}) %reduce-scatter.7.cloned.1.call-update) | async-done | bytes 589840 | tf_op jit(solution)/shard_map/reduce_scatter | solution.py:183
  187.8 5.7 all-to-all-start.1
  203.7 4.3 all-to-all-start
  208.1 7.2 %convolution_bitcast_fusion = f32[1536,512]{0,1:T(8,128)} fusion(bf16[512,1536]{1,0:T(8,128)(2,1)} %bitcast.237, bf16[1536,1536]{1,0:T(8,128)(2,1)} %param.11), kind=kOutput, calls=%fused_computation.24 | convolution fusion | flops 2415919104 | bytes 9437184 | tf_op jit(solution)/shard_map/dot_general | solution.py:185
  269.8 4.4 all-to-all-start.4
  274.2 4.2 bitcast_reduce_fusion
  284.1 6.0 all-to-all-start.5
  297.1 29.3 %all-to-all-done.5 = bf16[128,24,2,128]{3,1,2,0:T(8,128)(2,1)} async-done(((bf16[128,24,2,128]{3,1,2,0:T(8,128)(2,1)}), bf16[128,24,2,128]{3,1,2,0:T(8,128)(2,1)}, u32[]{:S(2)}, u32[]{:S(2)}) %all-to-all-start.5) | async-done | bytes 1572896 | tf_op jit(solution)/shard_map/all_to_all | solution.py:226
  338.1 12.2 %all-gather.12.cloned.1.call-done = bf16[1152,512]{1,0:T(8,128)(2,1)} async-done(((bf16[1152,128]{1,0:T(8,128)(2,1)}), bf16[1152,512]{1,0:T(8,128)(2,1)}) %all-gather.12.cloned.1.call-update) | async-done | bytes 1179664 | tf_op jit(solution)/shard_map/all_gather | solution.py:232
  350.3 5.2 fusion.109
  355.4 16.7 %all-gather.14.cloned.1.call-done = bf16[1536,512]{0,1:T(8,128)(2,1)} async-done(((bf16[1536,128]{0,1:T(8,128)(2,1)}), bf16[1536,512]{0,1:T(8,128)(2,1)}) %all-gather.14.cloned.1.call-update) | async-done | bytes 1572880 | tf_op jit(solution)/shard_map/all_gather | solution.py:233
  372.1 8.0 %convolution_add_fusion.1 = f32[512,1536]{1,0:T(8,128)} fusion(f32[512,1536]{1,0:T(8,128)} %fusion.109, bf16[1536,512]{0,1:T(8,128)(2,1)} %all-gather.14.cloned.1.call-done, bf16[1536,1536]{1,0:T(8,128)(2,1)} %param.11), kind=kOutput, calls=%fused_computation.26 | convolution fusion | flops 2416705536 | bytes 12582912 | tf_op jit(solution)/shard_map/dot_general | solution.py:238
  394.5 5.5 all-to-all-start.2
  403.2 4.1 all-to-all-done.2
  409.8 6.3 %all_gather.34 = bf16[384,512]{1,0:T(8,128)(2,1)S(1)} all-gather(bf16[384,128]{1,0:T(8,128)(2,1)S(1)} %reshape.183), channel_id=1, replica_groups=mesh['dp'=4,'mp'=8] {'dp'}, dimensions={1}, use_global_device_ids=true | all-gather | bytes 491520 | tf_op jit(solution)/shard_map/all_gather | solution.py:201
  421.7 5.3 fusion.107
  437.4 4.0 fusion.13
  452.3 5.9 add_convert_fusion
  458.2 5.0 add_convert_fusion.1
  465.5 4.0 fusion.5
  472.2 4.6 collective-permute-start.3
  476.8 6.3 %fusion.3 = bf16[1152,1536]{1,0:T(8,128)(2,1)} fusion(f32[1152,1536]{1,0:T(8,128)} %fusion.5, bf16[128,1536]{0,1:T(8,128)(2,1)} %bitcast.211, bf16[1152,512]{1,0:T(8,128)(2,1)} %all-gather.12.cloned.1.call-done), kind=kOutput, calls=%fused_computation.6 | convolution fusion | flops 460062720 | bytes 11304960 | tf_op jit(solution)/shard_map/dot_general | solution.py:147
  483.1 77.0 %reduce-scatter.11.cloned.1.call-done = f32[1,128,768]{2,1,0:T(8,128)} async-done(((f32[8,128,768]{2,1,0:T(8,128)}), f32[1,128,768]{2,1,0:T(8,128)}) %reduce-scatter.11.cloned.1.call-update) | async-done | bytes 393232 | tf_op jit(solution)/shard_map/reduce_scatter | solution.py:138
  560.1 4.5 collective-permute-start.1
  566.4 6.8 %psum.23 = f32[768]{0:T(1024)} all-reduce(f32[768]{0:T(1024)S(1)} %get-tuple-element.9), channel_id=1, replica_groups=mesh['dp'=4,'mp'=8] {'dp'}, use_global_device_ids=true, to_apply=%region_27.0 | all-reduce | flops 768 | bytes 6144 | tf_op jit(solution)/shard_map/psum | solution.py:249
  573.2 20.9 %all-reduce = (f32[128]{0:T(128)}, f32[128]{0:T(128)}) all-reduce(f32[128]{0:T(128)} %get-tuple-element.10, f32[128]{0:T(128)} %get-tuple-element.11), channel_id=1, replica_groups=mesh['dp'=4,'mp'=8] {'mp'}, use_global_device_ids=true, to_apply=%region_25.0 | all-reduce | flops 256 | bytes 2048 | tf_op jit(solution)/shard_map/psum | solution.py:243
  (223 shorter events, 189.8 us)
Async XLA Ops:
  7.2 110.9 %copy-start = (bf16[3,16,24,1536]{3,2,1,0:T(8,128)(2,1)S(1)}, bf16[3,16,24,1536]{3,2,1,0:T(8,128)(2,1)}, u32[]{:S(2)}) copy-start(bf16[3,16,24,1536]{3,2,1,0:T(8,128)(2,1)} %param.9) | copy-start | bytes 10616836
  7.2 61.2 %all-gather.18.cloned.1.call-start = ((), (), s32[]{:S(2)}) async-start(), calls=%async_computation.22 | async-start | bytes 1769472 | tf_op jit(solution)/shard_map/all_gather | solution.py:127
  7.2 3.4 collective-permute-start.2
  10.6 104.1 %all-gather.16.cloned.1.call-start = ((), (), s32[]{:S(2)}) async-start(), calls=%async_computation.21 | async-start | bytes 1769472 | tf_op jit(solution)/shard_map/all_gather | solution.py:127
  44.6 26.8 %copy-start.34 = (f32[128]{0:T(128)}, f32[128]{0:T(128)S(1)}, u32[]{:S(2)}) copy-start(f32[128]{0:T(128)S(1)} %broadcast_multiply_fusion.8) | copy-start | bytes 1540
  44.6 26.8 %copy-start.36 = (f32[128]{0:T(128)}, f32[128]{0:T(128)S(1)}, u32[]{:S(2)}) copy-start(f32[128]{0:T(128)S(1)} %add_rsqrt_fusion.2) | copy-start | bytes 1540
  45.7 1.3 collective-permute-start
  47.1 92.9 %reduce-scatter.13.cloned.1.call-start = ((), (), s32[]{:S(2)}) async-start(), calls=%async_computation.16 | async-start | bytes 983040 | tf_op jit(solution)/shard_map/reduce_scatter | solution.py:220
  74.6 101.7 %reduce-scatter.7.cloned.1.call-start = ((), (), s32[]{:S(2)}) async-start(), calls=%async_computation.12 | async-start | bytes 2949120 | tf_op jit(solution)/shard_map/reduce_scatter | solution.py:183
  122.9 211.6 %reduce-scatter.15.cloned.1.call-start = ((), (), s32[]{:S(2)}) async-start(), calls=%async_computation.18 | async-start | bytes 3932160 | tf_op jit(solution)/shard_map/reduce_scatter | solution.py:215
  149.0 38.8 %all-to-all-start.3 = ((bf16[8,2,3072]{2,1,0:T(2,128)(2,1)}), bf16[8,2,3072]{2,1,0:T(2,128)(2,1)}, u32[]{:S(2)}, u32[]{:S(2)}) async-start(bf16[8,2,3072]{2,1,0:T(2,128)(2,1)} %reshape.215), calls=%async_computation.7 | async-start | bytes 196608 | tf_op jit(solution)/shard_map/all_to_all | solution.py:222
  187.8 13.0 %all-to-all-start.1 = ((bf16[8,2,3072]{2,1,0:T(2,128)(2,1)}), bf16[8,2,3072]{2,1,0:T(2,128)(2,1)}, u32[]{:S(2)}, u32[]{:S(2)}) async-start(bf16[8,2,3072]{2,1,0:T(2,128)(2,1)} %reshape.211), calls=%async_computation.2 | async-start | bytes 196608 | tf_op jit(solution)/shard_map/all_to_all | solution.py:194
  203.7 40.6 %all-to-all-start = ((bf16[16,192,2,128]{3,2,0,1:T(2,128)(2,1)}), bf16[16,192,2,128]{3,2,0,1:T(2,128)(2,1)}, u32[]{:S(2)}, u32[]{:S(2)}) async-start(bf16[16,192,2,128]{3,2,0,1:T(2,128)(2,1)} %bitcast.205), calls=%async_computation.1 | async-start | bytes 3145728 | tf_op jit(solution)/shard_map/all_to_all | solution.py:195
  208.0 126.5 %reduce-scatter.9.cloned.1.call-start = ((), (), s32[]{:S(2)}) async-start(), calls=%async_computation.13 | async-start | bytes 3932160 | tf_op jit(solution)/shard_map/reduce_scatter | solution.py:188
  269.8 14.3 %all-to-all-start.4 = ((bf16[8,2,3072]{2,1,0:T(2,128)(2,1)}), bf16[8,2,3072]{2,1,0:T(2,128)(2,1)}, u32[]{:S(2)}, u32[]{:S(2)}) async-start(bf16[8,2,3072]{2,1,0:T(2,128)(2,1)} %reshape.217), calls=%async_computation.8 | async-start | bytes 196608 | tf_op jit(solution)/shard_map/all_to_all | solution.py:225
  284.1 42.3 %all-to-all-start.5 = ((bf16[128,24,2,128]{3,1,2,0:T(8,128)(2,1)}), bf16[128,24,2,128]{3,1,2,0:T(8,128)(2,1)}, u32[]{:S(2)}, u32[]{:S(2)}) async-start(bf16[128,24,2,128]{3,1,2,0:T(8,128)(2,1)} %copy.197), calls=%async_computation.9 | async-start | bytes 3145728 | tf_op jit(solution)/shard_map/all_to_all | solution.py:226
  290.1 60.2 %all-gather.12.cloned.1.call-start = ((), (), s32[]{:S(2)}) async-start(), calls=%async_computation.17 | async-start | bytes 1474560 | tf_op jit(solution)/shard_map/all_gather | solution.py:232
  334.4 37.7 %all-gather.14.cloned.1.call-start = ((), (), s32[]{:S(2)}) async-start(), calls=%async_computation.19 | async-start | bytes 1966080 | tf_op jit(solution)/shard_map/all_gather | solution.py:233
  337.2 84.6 %all-gather.10.cloned.1.call-start = ((), (), s32[]{:S(2)}) async-start(), calls=%async_computation.14 | async-start | bytes 1966080 | tf_op jit(solution)/shard_map/all_gather | solution.py:202
  337.9 134.3 %reduce-scatter.17.cloned.1.call-start = ((), (), s32[]{:S(2)}) async-start(), calls=%async_computation.20 | async-start | bytes 3538944 | tf_op jit(solution)/shard_map/reduce_scatter | solution.py:138
  390.4 9.7 %copy-start.7 = (bf16[1024,768]{1,0:T(8,128)(2,1)S(1)}, bf16[1024,768]{1,0:T(8,128)(2,1)}, u32[]{:S(2)}) copy-start(bf16[1024,768]{1,0:T(8,128)(2,1)} %all-gather.16.cloned.1.call-done) | copy-start | bytes 4718596
  394.5 12.8 %all-to-all-start.2 = ((bf16[8,2,3072]{2,1,0:T(2,128)(2,1)}), bf16[8,2,3072]{2,1,0:T(2,128)(2,1)}, u32[]{:S(2)}, u32[]{:S(2)}) async-start(bf16[8,2,3072]{2,1,0:T(2,128)(2,1)} %reshape.213), calls=%async_computation.3 | async-start | bytes 196608 | tf_op jit(solution)/shard_map/all_to_all | solution.py:198
  400.1 160.0 %reduce-scatter.11.cloned.1.call-start = ((), (), s32[]{:S(2)}) async-start(), calls=%async_computation.15 | async-start | bytes 3538944 | tf_op jit(solution)/shard_map/reduce_scatter | solution.py:138
  400.4 47.5 %copy-start.10 = (bf16[1,128,2,768]{1,3,2,0:T(8,128)(2,1)}, bf16[1,128,2,768]{1,3,2,0:T(8,128)(2,1)S(1)}, u32[]{:S(2)}) copy-start(bf16[1,128,2,768]{1,3,2,0:T(8,128)(2,1)S(1)} %copy.206) | copy-start | bytes 1179652
  403.2 12.9 %copy-start.11 = (bf16[1,128,2,768]{1,3,2,0:T(8,128)(2,1)S(1)}, bf16[1,128,2,768]{1,3,2,0:T(8,128)(2,1)}, u32[]{:S(2)}) copy-start(bf16[1,128,2,768]{1,3,2,0:T(8,128)(2,1)} %copy.210) | copy-start | bytes 1179652
  409.8 8.2 %copy-start.13 = (bf16[1,128,2,768]{1,3,2,0:T(8,128)(2,1)S(1)}, bf16[1,128,2,768]{1,3,2,0:T(8,128)(2,1)}, u32[]{:S(2)}) copy-start(bf16[1,128,2,768]{1,3,2,0:T(8,128)(2,1)} %copy.209) | copy-start | bytes 1179652
  416.1 11.0 %copy-start.17 = (bf16[384,512]{1,0:T(8,128)(2,1)}, bf16[384,512]{1,0:T(8,128)(2,1)S(1)}, u32[]{:S(2)}) copy-start(bf16[384,512]{1,0:T(8,128)(2,1)S(1)} %all_gather.34) | copy-start | bytes 1179652
  472.2 92.3 %copy-start.35 = (f32[128]{0:T(128)S(1)}, f32[128]{0:T(128)}, u32[]{:S(2)}) copy-start(f32[128]{0:T(128)} %copy-done.34) | copy-start | bytes 1540
  472.2 92.3 %copy-start.37 = (f32[128]{0:T(128)S(1)}, f32[128]{0:T(128)}, u32[]{:S(2)}) copy-start(f32[128]{0:T(128)} %copy-done.36) | copy-start | bytes 1540
  472.2 92.3 %collective-permute-start.3 = (f32[128,768]{1,0:T(8,128)}, f32[128,768]{1,0:T(8,128)}, u32[]{:S(2)}, u32[]{:S(2)}) collective-permute-start(f32[128,768]{1,0:T(8,128)} %bitcast.249), channel_id=1, source_target_pairs={{0,0},{1,1},{2,8},{3,9},{4,16},{5,17},{6,24},{7,25},{8,2},{9,3},{1... | collective-permute-start | bytes 1179656 | tf_op jit(solution)/shard_map/ppermute | solution.py:120
  476.8 120.9 %copy-start.1 = (bf16[3,16,24,1536]{3,2,1,0:T(8,128)(2,1)S(1)}, bf16[3,16,24,1536]{3,2,1,0:T(8,128)(2,1)}, u32[]{:S(2)}) copy-start(bf16[3,16,24,1536]{3,2,1,0:T(8,128)(2,1)} %param.9) | copy-start | bytes 10616836
  560.1 35.3 %collective-permute-start.1 = (f32[128,768]{1,0:T(8,128)}, f32[128,768]{1,0:T(8,128)}, u32[]{:S(2)}, u32[]{:S(2)}) collective-permute-start(f32[128,768]{1,0:T(8,128)} %bitcast.250), channel_id=1, source_target_pairs={{0,0},{1,1},{2,8},{3,9},{4,16},{5,17},{6,24},{7,25},{8,2},{9,3},{1... | collective-permute-start | bytes 1179656 | tf_op jit(solution)/shard_map/ppermute | solution.py:120
  (27 other events, 59.8 us)
Sparse Core Ops, SparseCore 0:
  10.7 57.5 all-gather.17
  70.5 44.1 all-gather.15
  117.9 22.0 reduce-scatter.12
  143.1 33.0 reduce-scatter.6
  179.2 37.9 reduce-scatter.14
  220.3 37.9 reduce-scatter.8
  334.6 15.6 all-gather.11
  352.4 19.6 all-gather.13
  374.3 19.6 all-gather.9
  398.0 74.2 reduce-scatter.16
  475.8 84.2 reduce-scatter.10
where the time goes:
time: 616 us; the launch traced here: 605 us
  waiting for transfers between devices  242 us (39%)
  local copies, waits for them, and re-layouts  110 us (18%)
  matrix products  97.6 us (16%)
  blocking collectives  65 us (11%)
  starting transfers between devices  45.8 us (7%)
  other arithmetic  29.7 us (5%)
  between operations  14.9 us (2%)
    reduce_scatter x2, waiting for transfers between devices, gather_quarter(): summed = lax.psum_scatter(pieces, 'mp', scatter_dimension=0, tiled=True)  79.7 us
    all_gather x2, waiting for transfers between devices, spread_quarter(): pieces = lax.all_gather(swap(block), 'mp', axis=0, tiled=False)  61.4 us
    dot_general x16, matrix products, blockwise_grad(): jnp.dot(left[:, block * rows:(block + 1) * rows], right[block * rows:(blo...  43.7 us
    all_gather x1, blocking collectives, shards(): lax.all_gather(jnp.stack([block_mean, block_m2]), 'mp', axis=0, tiled=False)  31 us
    all_to_all x1, waiting for transfers between devices, shards(): lax.all_to_all(pair_grad, 'mp', split_axis=0, concat_axis=1, tiled=True)  29.3 us
    unnamed x86, local copies, waits for them, and re-layouts  24.5 us
    reduce_scatter x1, waiting for transfers between devices, shards(): lax.psum_scatter(projected, 'dp', scatter_dimension=1, tiled=True)  21.7 us
    psum x1, blocking collectives, shards(): lax.psum((jnp.sum(scaled, axis=1), jnp.sum(scaled * normed, axis=1)), 'mp')  20.9 us
  transfers between devices with their start and end apart: 21, of which 12 were waited for; matrix products, arithmetic and copies ran while one was open for 37% of the time, Pallas kernels for 0%

commit v1 on v0

--- a/solution.py
+++ b/solution.py
@@ -229,8 +229,13 @@
         [query_local.reshape(1, head_slice, HEADS, ROWS), from_items(pair_local)], axis=0
     )
     proj_grad = proj_grad.reshape(3 * head_slice * HEADS, ROWS)
-    proj_grad_all = lax.all_gather(proj_grad, "dp", axis=1, tiled=True)
-    up_upstream_all = lax.all_gather(up_upstream, "dp", axis=1, tiled=True)
+    proj_grad_all, up_upstream_all = jnp.split(
+        lax.all_gather(
+            jnp.concatenate([proj_grad, up_upstream], axis=0), tiled=True, axis_name="dp", axis=1
+        ),
+        [proj_grad.shape[0]],
+        axis=0,
+    )
     qkv_grad = blockwise_grad(proj_grad_all, hidden_all, n_dp)
     up_grad = blockwise_grad(up_upstream_all, hidden_all, n_dp)
     input_partial = lax.dot_general(

time: 616 us -> 608 us (0.987)
  matrix products: 97.6 us -> 89.4 us
    all_gather x2 -> x1, waiting for transfers between devices: 28.8 us -> 23.6 us  [shards(): lax.all_gather(jnp.concatenate([proj_grad, up_upstream], axis=0), tiled=T...]
    unnamed x86 -> x78, local copies, waits for them, and re-layouts: 24.5 us -> 24.3 us
  transfers between devices with their start and end apart: 21 -> 20, of which waited for: 12 -> 11; matrix products, arithmetic and copies ran while one was open for 37% -> 36% of each run, Pallas kernels for 0% -> 0%
where the time goes in v1:
time: 608 us; the launch traced here: 596 us
  waiting for transfers between devices  236 us (39%)
  local copies, waits for them, and re-layouts  114 us (19%)
  matrix products  89.4 us (15%)
  blocking collectives  64.9 us (11%)
  starting transfers between devices  45.7 us (8%)
  other arithmetic  31.6 us (5%)
  between operations  15.2 us (2%)
    reduce_scatter x2, waiting for transfers between devices, gather_quarter(): summed = lax.psum_scatter(pieces, 'mp', scatter_dimension=0, tiled=True)  80.1 us
    all_gather x2, waiting for transfers between devices, spread_quarter(): pieces = lax.all_gather(swap(block), 'mp', axis=0, tiled=False)  61.4 us
    dot_general x16, matrix products, blockwise_grad(): jnp.dot(left[:, block * rows:(block + 1) * rows], right[block * rows:(blo...  38.8 us
    all_gather x1, blocking collectives, shards(): lax.all_gather(jnp.stack([block_mean, block_m2]), 'mp', axis=0, tiled=False)  31 us
    all_to_all x1, waiting for transfers between devices, shards(): lax.all_to_all(pair_grad, 'mp', split_axis=0, concat_axis=1, tiled=True)  26.7 us
    unnamed x78, local copies, waits for them, and re-layouts  24.3 us
    all_gather x1, waiting for transfers between devices, shards(): lax.all_gather(jnp.concatenate([proj_grad, up_upstream], axis=0), tiled=T...  23.6 us
    reduce_scatter x1, waiting for transfers between devices, shards(): lax.psum_scatter(projected, 'dp', scatter_dimension=1, tiled=True)  21.7 us
  transfers between devices with their start and end apart: 20, of which 11 were waited for; matrix products, arithmetic and copies ran while one was open for 36% of the time, Pallas kernels for 0%

profile of v1, /device:TPU:0, one launch (start us, length us, event | category | flops | bytes accessed | tf_op | source)
XLA Modules:
  0.0 596.5 jit_solution(5633966911684042112)
XLA Ops:
  13.5 31.0 %all-gather.3 = f32[8,2,128]{2,1,0:T(2,128)S(1)} all-gather(f32[1,2,128]{2,1,0:T(2,128)S(1)} %maximum_bitcast_fusion), channel_id=2, replica_groups=mesh['dp'=4,'mp'=8] {'mp'}, dimensions={0}, use_global_device_ids=true | all-gather | bytes 9216 | tf_op jit(solution)/shard_map/all_gather | solution.py:170
  47.2 21.2 %all-gather.15.cloned.1.call-done = bf16[1024,768]{1,0:T(8,128)(2,1)} async-done(((bf16[128,768]{1,0:T(8,128)(2,1)}), bf16[1024,768]{1,0:T(8,128)(2,1)}) %all-gather.15.cloned.1.call-update) | async-done | bytes 1572880 | tf_op jit(solution)/shard_map/all_gather | solution.py:127
  74.6 40.2 %all-gather.13.cloned.1.call-done = bf16[1024,768]{1,0:T(8,128)(2,1)} async-done(((bf16[128,768]{1,0:T(8,128)(2,1)}), bf16[1024,768]{1,0:T(8,128)(2,1)}) %all-gather.13.cloned.1.call-update) | async-done | bytes 1572880 | tf_op jit(solution)/shard_map/all_gather | solution.py:127
  123.0 7.3 %fusion.112 = f32[1536,512]{0,1:T(8,128)} fusion(bf16[1536,1536]{1,0:T(8,128)(2,1)} %param.12, bf16[512,1536]{1,0:T(8,128)(2,1)} %bitcast.237), kind=kOutput, calls=%fused_computation.165 | convolution fusion | flops 2415919104 | bytes 9437184 | tf_op jit(solution)/shard_map/dot_general | solution.py:212
  130.3 9.7 %reduce-scatter.13.cloned.1.call-done = f32[384,128]{1,0:T(8,128)} async-done(((f32[384,512]{1,0:T(8,128)}), f32[384,128]{1,0:T(8,128)}) %reduce-scatter.13.cloned.1.call-update) | async-done | bytes 196624 | tf_op jit(solution)/shard_map/reduce_scatter | solution.py:220
  149.0 5.5 all-to-all-start.3
  154.5 21.7 %reduce-scatter.7.cloned.1.call-done = f32[1152,128]{0,1:T(8,128)} async-done(((f32[1152,512]{0,1:T(8,128)}), f32[1152,128]{0,1:T(8,128)}) %reduce-scatter.7.cloned.1.call-update) | async-done | bytes 589840 | tf_op jit(solution)/shard_map/reduce_scatter | solution.py:183
  187.8 5.7 all-to-all-start.1
  203.7 4.3 all-to-all-start
  208.1 7.2 %convolution_bitcast_fusion = f32[1536,512]{0,1:T(8,128)} fusion(bf16[512,1536]{1,0:T(8,128)(2,1)} %bitcast.235, bf16[1536,1536]{1,0:T(8,128)(2,1)} %param.11), kind=kOutput, calls=%fused_computation.24 | convolution fusion | flops 2415919104 | bytes 9437184 | tf_op jit(solution)/shard_map/dot_general | solution.py:185
  240.1 4.2 all-to-all-done
  269.8 4.4 all-to-all-start.4
  274.2 4.2 bitcast_reduce_fusion
  284.0 6.0 all-to-all-start.5
  299.6 26.7 %all-to-all-done.5 = bf16[128,24,2,128]{3,1,2,0:T(8,128)(2,1)} async-done(((bf16[128,24,2,128]{3,1,2,0:T(8,128)(2,1)}), bf16[128,24,2,128]{3,1,2,0:T(8,128)(2,1)}, u32[]{:S(2)}, u32[]{:S(2)}) %all-to-all-start.5) | async-done | bytes 1572896 | tf_op jit(solution)/shard_map/all_to_all | solution.py:226
  339.1 23.6 %all-gather.11.cloned.1.call-done = bf16[2688,512]{0,1:T(8,128)(2,1)} async-done(((bf16[2688,128]{0,1:T(8,128)(2,1)}), bf16[2688,512]{0,1:T(8,128)(2,1)}) %all-gather.11.cloned.1.call-update) | async-done | bytes 2752528 | tf_op jit(solution)/shard_map/all_gather | solution.py:233
  366.3 6.7 %convolution_add_fusion.1 = f32[512,1536]{1,0:T(8,128)} fusion(f32[512,1536]{1,0:T(8,128)S(1)} %fusion.30, bf16[1536,1536]{1,0:T(8,128)(2,1)} %param.11, bf16[2688,512]{0,1:T(8,128)(2,1)S(1)} %copy-done.7), kind=kOutput, calls=%fused_computation.26 | convolution fusion | flops 2416705536 | bytes 12582912 | tf_op jit(solution)/shard_map/dot_general | solution.py:243
  390.2 5.5 all-to-all-start.2
  398.9 5.5 all-to-all-done.2
  406.9 6.4 %all_gather.31 = bf16[384,512]{1,0:T(8,128)(2,1)S(1)} all-gather(bf16[384,128]{1,0:T(8,128)(2,1)S(1)} %reshape.183), channel_id=1, replica_groups=mesh['dp'=4,'mp'=8] {'dp'}, dimensions={1}, use_global_device_ids=true | all-gather | bytes 491520 | tf_op jit(solution)/shard_map/all_gather | solution.py:201
  418.9 5.1 fusion.110
  426.7 3.9 reshape.185
  434.4 4.1 fusion.13
  442.8 4.1 add_convert_fusion
  453.6 4.0 fusion.5
  457.6 3.9 add_convert_fusion.1
  464.6 4.6 collective-permute-start.3
  469.2 6.3 %fusion.3 = bf16[1152,1536]{1,0:T(8,128)(2,1)} fusion(f32[1152,1536]{1,0:T(8,128)} %fusion.5, bf16[128,1536]{0,1:T(8,128)(2,1)} %bitcast.209, bf16[2688,512]{0,1:T(8,128)(2,1)} %all-gather.11.cloned.1.call-done), kind=kOutput, calls=%fused_computation.6 | convolution fusion | flops 460062720 | bytes 11304960 | tf_op jit(solution)/shard_map/dot_general | solution.py:147
  475.4 77.0 %reduce-scatter.11.cloned.1.call-done = f32[1,128,768]{2,1,0:T(8,128)} async-done(((f32[8,128,768]{2,1,0:T(8,128)}), f32[1,128,768]{2,1,0:T(8,128)}) %reduce-scatter.11.cloned.1.call-update) | async-done | bytes 393232 | tf_op jit(solution)/shard_map/reduce_scatter | solution.py:138
  552.4 4.5 collective-permute-start.1
  558.7 6.8 %psum.23 = f32[768]{0:T(1024)} all-reduce(f32[768]{0:T(1024)S(1)} %get-tuple-element.9), channel_id=1, replica_groups=mesh['dp'=4,'mp'=8] {'dp'}, use_global_device_ids=true, to_apply=%region_27.0 | all-reduce | flops 768 | bytes 6144 | tf_op jit(solution)/shard_map/psum | solution.py:254
  565.5 20.7 %all-reduce = (f32[128]{0:T(128)}, f32[128]{0:T(128)S(1)}) all-reduce(f32[128]{0:T(128)} %get-tuple-element.10, f32[128]{0:T(128)} %get-tuple-element.11), channel_id=1, replica_groups=mesh['dp'=4,'mp'=8] {'mp'}, use_global_device_ids=true, to_apply=%region_25.0 | all-reduce | flops 256 | bytes 2048 | tf_op jit(solution)/shard_map/psum | solution.py:248
  (214 shorter events, 189.3 us)
Async XLA Ops:
  7.2 110.9 %copy-start = (bf16[3,16,24,1536]{3,2,1,0:T(8,128)(2,1)S(1)}, bf16[3,16,24,1536]{3,2,1,0:T(8,128)(2,1)}, u32[]{:S(2)}) copy-start(bf16[3,16,24,1536]{3,2,1,0:T(8,128)(2,1)} %param.9) | copy-start | bytes 10616836
  7.2 61.2 %all-gather.15.cloned.1.call-start = ((), (), s32[]{:S(2)}) async-start(), calls=%async_computation.21 | async-start | bytes 1769472 | tf_op jit(solution)/shard_map/all_gather | solution.py:127
  7.2 3.4 collective-permute-start.2
  10.6 104.1 %all-gather.13.cloned.1.call-start = ((), (), s32[]{:S(2)}) async-start(), calls=%async_computation.20 | async-start | bytes 1769472 | tf_op jit(solution)/shard_map/all_gather | solution.py:127
  45.7 1.3 collective-permute-start
  47.1 92.9 %reduce-scatter.13.cloned.1.call-start = ((), (), s32[]{:S(2)}) async-start(), calls=%async_computation.16 | async-start | bytes 983040 | tf_op jit(solution)/shard_map/reduce_scatter | solution.py:220
  74.5 101.7 %reduce-scatter.7.cloned.1.call-start = ((), (), s32[]{:S(2)}) async-start(), calls=%async_computation.12 | async-start | bytes 2949120 | tf_op jit(solution)/shard_map/reduce_scatter | solution.py:183
  122.9 167.1 %reduce-scatter.15.cloned.1.call-start = ((), (), s32[]{:S(2)}) async-start(), calls=%async_computation.17 | async-start | bytes 3932160 | tf_op jit(solution)/shard_map/reduce_scatter | solution.py:215
  149.0 38.8 %all-to-all-start.3 = ((bf16[8,2,3072]{2,1,0:T(2,128)(2,1)}), bf16[8,2,3072]{2,1,0:T(2,128)(2,1)}, u32[]{:S(2)}, u32[]{:S(2)}) async-start(bf16[8,2,3072]{2,1,0:T(2,128)(2,1)} %reshape.215), calls=%async_computation.7 | async-start | bytes 196608 | tf_op jit(solution)/shard_map/all_to_all | solution.py:222
  187.8 13.0 %all-to-all-start.1 = ((bf16[8,2,3072]{2,1,0:T(2,128)(2,1)}), bf16[8,2,3072]{2,1,0:T(2,128)(2,1)}, u32[]{:S(2)}, u32[]{:S(2)}) async-start(bf16[8,2,3072]{2,1,0:T(2,128)(2,1)} %reshape.211), calls=%async_computation.2 | async-start | bytes 196608 | tf_op jit(solution)/shard_map/all_to_all | solution.py:194
  203.7 40.6 %all-to-all-start = ((bf16[16,192,2,128]{3,2,0,1:T(2,128)(2,1)}), bf16[16,192,2,128]{3,2,0,1:T(2,128)(2,1)}, u32[]{:S(2)}, u32[]{:S(2)}) async-start(bf16[16,192,2,128]{3,2,0,1:T(2,128)(2,1)} %bitcast.203), calls=%async_computation.1 | async-start | bytes 3145728 | tf_op jit(solution)/shard_map/all_to_all | solution.py:195
  208.0 82.0 %reduce-scatter.9.cloned.1.call-start = ((), (), s32[]{:S(2)}) async-start(), calls=%async_computation.13 | async-start | bytes 3932160 | tf_op jit(solution)/shard_map/reduce_scatter | solution.py:188
  269.8 14.2 %all-to-all-start.4 = ((bf16[8,2,3072]{2,1,0:T(2,128)(2,1)}), bf16[8,2,3072]{2,1,0:T(2,128)(2,1)}, u32[]{:S(2)}, u32[]{:S(2)}) async-start(bf16[8,2,3072]{2,1,0:T(2,128)(2,1)} %reshape.217), calls=%async_computation.8 | async-start | bytes 196608 | tf_op jit(solution)/shard_map/all_to_all | solution.py:225
  284.0 42.3 %all-to-all-start.5 = ((bf16[128,24,2,128]{3,1,2,0:T(8,128)(2,1)}), bf16[128,24,2,128]{3,1,2,0:T(8,128)(2,1)}, u32[]{:S(2)}, u32[]{:S(2)}) async-start(bf16[128,24,2,128]{3,1,2,0:T(8,128)(2,1)} %copy.201), calls=%async_computation.9 | async-start | bytes 3145728 | tf_op jit(solution)/shard_map/all_to_all | solution.py:226
  290.0 72.7 %all-gather.11.cloned.1.call-start = ((), (), s32[]{:S(2)}) async-start(), calls=%async_computation.18 | async-start | bytes 3440640 | tf_op jit(solution)/shard_map/all_gather | solution.py:233
  338.1 80.8 %all-gather.9.cloned.1.call-start = ((), (), s32[]{:S(2)}) async-start(), calls=%async_computation.14 | async-start | bytes 1966080 | tf_op jit(solution)/shard_map/all_gather | solution.py:202
  338.8 125.7 %reduce-scatter.17.cloned.1.call-start = ((), (), s32[]{:S(2)}) async-start(), calls=%async_computation.19 | async-start | bytes 3538944 | tf_op jit(solution)/shard_map/reduce_scatter | solution.py:138
  381.2 5.8 copy-start.3
  382.1 13.7 %copy-start.6 = (bf16[1024,768]{1,0:T(8,128)(2,1)S(1)}, bf16[1024,768]{1,0:T(8,128)(2,1)}, u32[]{:S(2)}) copy-start(bf16[1024,768]{1,0:T(8,128)(2,1)} %all-gather.13.cloned.1.call-done) | copy-start | bytes 4718596
  390.2 14.2 %all-to-all-start.2 = ((bf16[8,2,3072]{2,1,0:T(2,128)(2,1)}), bf16[8,2,3072]{2,1,0:T(2,128)(2,1)}, u32[]{:S(2)}, u32[]{:S(2)}) async-start(bf16[8,2,3072]{2,1,0:T(2,128)(2,1)} %reshape.213), calls=%async_computation.3 | async-start | bytes 196608 | tf_op jit(solution)/shard_map/all_to_all | solution.py:198
  395.7 156.7 %reduce-scatter.11.cloned.1.call-start = ((), (), s32[]{:S(2)}) async-start(), calls=%async_computation.15 | async-start | bytes 3538944 | tf_op jit(solution)/shard_map/reduce_scatter | solution.py:138
  396.1 50.9 %copy-start.10 = (bf16[1,128,2,768]{1,3,2,0:T(8,128)(2,1)}, bf16[1,128,2,768]{1,3,2,0:T(8,128)(2,1)S(1)}, u32[]{:S(2)}) copy-start(bf16[1,128,2,768]{1,3,2,0:T(8,128)(2,1)S(1)} %copy.211) | copy-start | bytes 1179652
  397.0 16.3 %copy-start.11 = (bf16[1,128,2,768]{1,3,2,0:T(8,128)(2,1)S(1)}, bf16[1,128,2,768]{1,3,2,0:T(8,128)(2,1)}, u32[]{:S(2)}) copy-start(bf16[1,128,2,768]{1,3,2,0:T(8,128)(2,1)} %copy.215) | copy-start | bytes 1179652
  406.4 8.8 %copy-start.13 = (bf16[1,128,2,768]{1,3,2,0:T(8,128)(2,1)S(1)}, bf16[1,128,2,768]{1,3,2,0:T(8,128)(2,1)}, u32[]{:S(2)}) copy-start(bf16[1,128,2,768]{1,3,2,0:T(8,128)(2,1)} %copy.214) | copy-start | bytes 1179652
  413.3 10.7 %copy-start.17 = (bf16[384,512]{1,0:T(8,128)(2,1)}, bf16[384,512]{1,0:T(8,128)(2,1)S(1)}, u32[]{:S(2)}) copy-start(bf16[384,512]{1,0:T(8,128)(2,1)S(1)} %all_gather.31) | copy-start | bytes 1179652
  418.9 5.1 copy-start.26
  442.8 4.2 copy-start.8
  464.6 92.3 %copy-start.31 = (f32[128]{0:T(128)S(1)}, f32[128]{0:T(128)}, u32[]{:S(2)}) copy-start(f32[128]{0:T(128)} %copy-done.30) | copy-start | bytes 1540
  464.6 92.3 %copy-start.33 = (f32[128]{0:T(128)S(1)}, f32[128]{0:T(128)}, u32[]{:S(2)}) copy-start(f32[128]{0:T(128)} %copy-done.32) | copy-start | bytes 1540
  464.6 92.3 %collective-permute-start.3 = (f32[128,768]{1,0:T(8,128)}, f32[128,768]{1,0:T(8,128)}, u32[]{:S(2)}, u32[]{:S(2)}) collective-permute-start(f32[128,768]{1,0:T(8,128)} %bitcast.247), channel_id=1, source_target_pairs={{0,0},{1,1},{2,8},{3,9},{4,16},{5,17},{6,24},{7,25},{8,2},{9,3},{1... | collective-permute-start | bytes 1179656 | tf_op jit(solution)/shard_map/ppermute | solution.py:120
  469.2 120.0 %copy-start.1 = (bf16[3,16,24,1536]{3,2,1,0:T(8,128)(2,1)S(1)}, bf16[3,16,24,1536]{3,2,1,0:T(8,128)(2,1)}, u32[]{:S(2)}) copy-start(bf16[3,16,24,1536]{3,2,1,0:T(8,128)(2,1)} %param.9) | copy-start | bytes 10616836
  552.4 34.5 %collective-permute-start.1 = (f32[128,768]{1,0:T(8,128)}, f32[128,768]{1,0:T(8,128)}, u32[]{:S(2)}, u32[]{:S(2)}) collective-permute-start(f32[128,768]{1,0:T(8,128)} %bitcast.248), channel_id=1, source_target_pairs={{0,0},{1,1},{2,8},{3,9},{4,16},{5,17},{6,24},{7,25},{8,2},{9,3},{1... | collective-permute-start | bytes 1179656 | tf_op jit(solution)/shard_map/ppermute | solution.py:120
  (22 other events, 46.2 us)
Sparse Core Ops, SparseCore 0:
  10.7 57.5 all-gather.14
  70.5 44.1 all-gather.12
  117.9 22.0 reduce-scatter.12
  143.1 33.0 reduce-scatter.6
  179.2 37.9 reduce-scatter.14
  220.3 37.9 reduce-scatter.8
  338.2 24.4 all-gather.10
  364.8 19.6 all-gather.8
  388.7 75.8 reduce-scatter.16
  468.0 84.3 reduce-scatter.10
